TPU v7x, 256 devices: a whole 4x4x8 slice. The times are simulated.
256 devices in a mesh: tm: 16 (over z, x_hi), height: 4 (over x_lo, core), mp: 4 (over y).
Axes of the slice: x: 4 (x_hi: 2, x_lo: 2; x = x_hi * 2 + x_lo), y: 4, z: 8, core: 2. Of those that a mesh axis runs over, the one named last changes fastest.
Arguments:
- image_q: bfloat16 [16, 4, 384, 3072], P('tm', 'height', None, 'mp'), may hold values from -8 to 8
- image_kv: bfloat16 [16, 4, 2, 384, 3072], P('tm', 'height', None, None, 'mp'), may hold values from -8 to 8
- text_kv: bfloat16 [2, 256, 3072], P(None, 'tm', 'mp'), may hold values from -8 to 8
- residual: bfloat16 [16, 4, 384, 3072], P('tm', 'height', None, 'mp'), may hold values from -3 to 3
- out_weight: bfloat16 [3072, 3072], P('mp'), may hold values from -0.109375 to 0.109375
- out_gate: float32 [3072], P('mp'), may hold values from 0.5 to 2
- head_reach: int32 [24, 2], P('mp'), may hold values from 0 to 1, as said below
- tile_extent: int32 [2, 16, 4], replicated, may hold values from 1 to 8, as said below
Outputs:
- updated_tokens: bfloat16 [16, 4, 384, 3072], P('tm', 'height', None, 'mp')
Inputs may be any that keep to these rules, and one draw needn't show every extreme that they name: `head_reach`: in each column exactly 16 heads have reach 1, the others 0. `tile_extent`: valid frames are 6 except in the last tile row along time, where they are below 6; valid rows are 8 except in the last tile row along height, where they are below 8.
All inputs are finite; a program needn't handle non-finite values.
Results may differ from a plain program's by a relative error of at most 0.015.
Values may be sent and summed in bfloat16 or wider, within the bound.
No kernel may reach another device: no remote copies, remote signals or barrier semaphores. Data moves between devices by JAX's collectives and lax.ppermute only.
A program may use at most 128 MiB of HBM per device.

v0:
```python
import math
import jax
import jax.numpy as jnp
from jax import lax
from jax.sharding import PartitionSpec as P

HD = 128
TXT = 256
TILE_F = 6
TILE_R = 8
TILE_C = 8


def with_halo(array, sides, width):
    for axis, dim in sides:
        devices, length = (lax.axis_size(axis), array.shape[dim])
        up = [(i, (i + 1) % devices) for i in range(devices - 1)]
        down = [(j, i) for i, j in up]
        last = lax.slice_in_dim(array, length - width, length, axis=dim)
        leading = lax.slice_in_dim(array, 0, width, axis=dim)
        before = lax.ppermute(last, axis, up)
        after = lax.ppermute(leading, axis, down)
        array = jnp.concatenate([before, array, after], axis=dim)
    return array


def token_masks(extent_pair):
    positions = jnp.arange(TILE_F * TILE_R * TILE_C, dtype=jnp.int32)
    frame_of = positions // (TILE_R * TILE_C)
    row_of = positions // TILE_C % TILE_R
    frame_ok = frame_of < extent_pair[0][..., None]
    row_ok = row_of < extent_pair[1][..., None]
    return jnp.logical_and(frame_ok, row_ok)


def extend_tiles(image_kv):
    return with_halo(image_kv, (("tm", 0), ("height", 1)), 1)


def per_device(image_q, image_kv, text_kv, residual, out_weight, out_gate, head_reach, tile_extent):
    tiles_local = image_q.shape[0]
    tile_len = image_q.shape[2]
    col_width = image_q.shape[3]
    heads_here = col_width // HD
    text_both = lax.all_gather(text_kv, "tm", axis=1, tiled=True)
    extended = extend_tiles(image_kv)
    time_start = lax.axis_index("tm") * tiles_local
    height_start = lax.axis_index("height")
    zero_index = jnp.int32(0)
    padded_ext = jnp.pad(tile_extent, ((0, 0), (1, 1), (1, 1)))
    local_ext = lax.dynamic_slice(
        padded_ext, (zero_index, time_start, height_start), (2, tiles_local + 2, 3)
    )
    key_valid = token_masks(local_ext)
    flat_valid = key_valid[1:-1, 1]
    flat_q = image_q.reshape(tiles_local, tile_len, col_width)
    offsets = jnp.abs(jnp.arange(3, dtype=jnp.int32) - 1)
    scale_factor = 1.0 / math.sqrt(HD)

    def one_tile(tile_index):
        key_rows = jnp.concatenate([extended[:, :, 0].reshape(-1, col_width), text_both[0]], axis=0)
        value_rows = jnp.concatenate(
            [extended[:, :, 1].reshape(-1, col_width), text_both[1]], axis=0
        )
        queries = lax.dynamic_index_in_dim(flat_q, tile_index, 0, keepdims=False)

        def one_head(packed):
            head_id, reaches = packed
            column_start = head_id * HD
            q_head = lax.dynamic_slice_in_dim(queries, column_start, HD, 1)
            k_head = lax.dynamic_slice_in_dim(key_rows, column_start, HD, 1)
            v_head = lax.dynamic_slice_in_dim(value_rows, column_start, HD, 1)
            image_ok = jnp.logical_and(key_valid, offsets[:, None, None] <= reaches[0])
            image_ok = jnp.logical_and(image_ok, offsets[None, :, None] <= reaches[1])
            allowed = jnp.concatenate([image_ok.reshape(-1), jnp.ones((TXT,), jnp.bool_)])
            scores = (
                lax.dot_general(
                    q_head, k_head, (((1,), (1,)), ((), ())), preferred_element_type=jnp.float32
                )
                * scale_factor
            )
            masked = jnp.where(allowed[None, :], scores, -1e30)
            top_score = jnp.max(masked, axis=1, keepdims=True)
            weights = jnp.where(allowed[None, :], jnp.exp(masked - top_score), 0.0)
            row_total = jnp.sum(weights, axis=1, keepdims=True)
            return (
                jnp.dot(weights.astype(jnp.bfloat16), v_head, preferred_element_type=jnp.float32)
                / row_total
            )

        per_head = lax.map(one_head, (jnp.arange(heads_here, dtype=jnp.int32), head_reach))
        joined = jnp.transpose(per_head, (1, 0, 2)).reshape(tile_len, col_width)
        valid_rows = lax.dynamic_index_in_dim(flat_valid, tile_index, 0, keepdims=False)
        return jnp.where(valid_rows[:, None], joined, 0.0).astype(jnp.bfloat16)

    attended = lax.map(one_tile, jnp.arange(tiles_local, dtype=jnp.int32))
    projected = jnp.dot(
        attended.reshape(-1, col_width), out_weight, preferred_element_type=jnp.float32
    )
    summed = lax.psum_scatter(
        projected.reshape(tiles_local, 1, tile_len, -1).astype(jnp.bfloat16),
        "mp",
        scatter_dimension=3,
        tiled=True,
    ).astype(jnp.float32)
    return (residual.astype(jnp.float32) + out_gate * summed).astype(jnp.bfloat16)


def solution(mesh):
    return jax.shard_map(
        per_device,
        mesh=mesh,
        in_specs=(
            P("tm", "height", None, "mp"),
            P("tm", "height", None, None, "mp"),
            P(None, "tm", "mp"),
            P("tm", "height", None, "mp"),
            P("mp", None),
            P("mp"),
            P("mp", None),
            P(),
        ),
        out_specs=P("tm", "height", None, "mp"),
        check_vma=False,
    )
```

profile of v0, /device:TPU:1, one launch (start us, length us, event | category | flops | bytes accessed | tf_op | source)
XLA Modules:
  0.0 288.8 jit_solution(14104560325803142447)
XLA Ops:
  6.5 5.7 %collective-permute-start = (bf16[1,1,2,384,768]{4,3,2,1,0:T(8,128)(2,1)}, bf16[1,1,2,384,768]{4,3,2,1,0:T(8,128)(2,1)S(1)}, u32[]{:S(2)}, u32[]{:S(2)}) collective-permute-start(bf16[1,1,2,384,768]{4,3,2,1,0:T(8,128)(2,1)} %param.11), channel_id=1, source_target_pairs={{0,16},{16,32},{32,48},{48,64},{64,80},{80,96},{96,112},{112,128},... | collective-permute-start | bytes 3538952 | tf_op jit(solution)/shard_map/ppermute | solution.py:21
  13.5 48.8 %collective-permute-done = bf16[1,1,2,384,768]{4,3,2,1,0:T(8,128)(2,1)S(1)} collective-permute-done((bf16[1,1,2,384,768]{4,3,2,1,0:T(8,128)(2,1)}, bf16[1,1,2,384,768]{4,3,2,1,0:T(8,128)(2,1)S(1)}, u32[]{:S(2)}, u32[]{:S(2)}) %collective-permute-start) | collective-permute-done | bytes 1179680 | tf_op jit(solution)/shard_map/ppermute | solution.py:21
  63.9 3.7 %collective-permute-start.2 = (bf16[3,1,2,384,768]{4,3,2,1,0:T(8,128)(2,1)S(1)}, bf16[3,1,2,384,768]{4,3,2,1,0:T(8,128)(2,1)}, u32[]{:S(2)}, u32[]{:S(2)}) collective-permute-start(bf16[3,1,2,384,768]{4,3,2,1,0:T(8,128)(2,1)S(1)} %constant_dynamic-update-slice_fusion.1), channel_id=1, source_target_pairs={{0,4},{4,8},{8,12},{1,5},{5,9},{9,13},{2,6},{6,10},{10,14},{3,7},{... | collective-permute-start | bytes 10616840 | tf_op jit(solution)/shard_map/ppermute | solution.py:21
  67.6 2.8 collective-permute-start.3
  73.6 76.8 %all_gather.3 = bf16[2,256,768]{2,1,0:T(8,128)(2,1)S(1)} all-gather(bf16[2,16,768]{2,1,0:T(8,128)(2,1)} %param.12), channel_id=1, replica_groups=mesh['tm'=16,'height'=4,'mp'=4] {'tm'}, dimensions={1}, use_global_device_ids=true | all-gather | bytes 835584 | tf_op jit(solution)/shard_map/all_gather | solution.py:45
  151.4 8.2 %pad_maximum_fusion = bf16[3,3,2,384,768]{4,3,2,1,0:T(8,128)(2,1)} fusion(bf16[3,1,2,384,768]{4,3,2,1,0:T(8,128)(2,1)} %collective-permute-done.3, bf16[3,1,2,384,768]{4,3,2,1,0:T(8,128)(2,1)S(1)} %constant_dynamic-update-slice_fusion.1, bf16[3,1,2,384,768]{4,3,2,1,0:T(8,128)(2,1)} %collective-permute-done.2), kind=kLoop, calls=%fused_computation.26 | loop fusion | flops 10616832 | bytes 21233664 | tf_op jit(solution)/shard_map/concatenate | solution.py:23
  159.6 9.0 %fusion.37 = (bf16[3,3,1,384,768]{4,3,2,1,0:T(8,128)(2,1)}, bf16[3,3,1,384,768]{4,3,2,1,0:T(8,128)(2,1)}) fusion(bf16[3,3,2,384,768]{4,3,2,1,0:T(8,128)(2,1)} %pad_maximum_fusion), kind=kLoop, calls=%fused_computation.60 | loop fusion | bytes 21233664 | tf_op jit(solution)/shard_map/while/body/eval_jaxpr/slice | solution.py:63
  168.6 9.5 %pad_maximum_fusion.1 = (bf16[3712,768]{1,0:T(8,128)(2,1)}, bf16[3712,768]{1,0:T(8,128)(2,1)}) fusion(bf16[256,768]{1,0:T(8,128)(2,1)S(1)} %copy-done.1, bf16[3456,768]{1,0:T(8,128)(2,1)} %bitcast.33, bf16[256,768]{1,0:T(8,128)(2,1)S(1)} %copy-done, bf16[3456,768]{1,0:T(8,128)(2,1)} %bitcast.32), kind=kLoop, calls=%fused_computation.27 | loop fusion | flops 22806528 | bytes 22806528 | tf_op jit(solution)/shard_map/while/body/eval_jaxpr/concatenate | solution.py:61
  178.1 54.3 %while.19 = (s32[]{:T(128)}, bf16[6,384,128]{1,2,0:T(8,128)(2,1)S(1)}, s32[6,2]{0,1:T(2,128)S(1)}, s32[6]{0:T(128)S(1)}, bf16[384,768]{1,0:T(8,128)(2,1)}, /*ind...) while((s32[]{:T(128)}, ...), condition=%wide.region_3.4_spmd.clone.clone, body=%wide.region_0.3_spmd.clone.clone.sunk | while | flops 742752384 | bytes 19636056 | solution.py:91
  181.3 2.4 fusion.53
  184.8 2.2 fusion.55
  190.3 2.4 fusion.53
  193.9 2.2 fusion.55
  199.4 2.4 fusion.53
  202.9 2.2 fusion.55
  208.4 2.4 fusion.53
  212.0 2.2 fusion.55
  217.5 2.4 fusion.53
  221.0 2.2 fusion.55
  226.5 2.4 fusion.53
  230.1 2.2 fusion.55
  232.6 5.9 %fusion.27 = bf16[1,1,384,3072]{3,2,1,0:T(8,128)(2,1)} fusion(bf16[384,768]{0,1:T(8,128)(2,1)S(1)} %fusion.28, bf16[768,3072]{1,0:T(8,128)(2,1)} %param.14), kind=kOutput, calls=%fused_computation.30 | convolution fusion | flops 1813118976 | bytes 7667712 | tf_op jit(solution)/shard_map/dot_general | solution.py:97
  238.5 41.4 %reduce-scatter.2.cloned.1.call-done = bf16[1,1,384,768]{3,2,1,0:T(8,128)(2,1)} async-done(((bf16[1,1,384,3072]{3,2,1,0:T(8,128)(2,1)}), bf16[1,1,384,768]{3,2,1,0:T(8,128)(2,1)}) %reduce-scatter.2.cloned.1.call-update) | async-done | bytes 589840 | tf_op jit(solution)/shard_map/reduce_scatter | solution.py:100
  279.9 2.1 add_convert_fusion
  (96 shorter events, 30.0 us)
Async XLA Ops:
  6.5 63.9 %copy-start.6 = (s32[2,16,4]{1,2,0:T(4,128)S(1)}, s32[2,16,4]{1,2,0:T(4,128)}, u32[]{:S(2)}) copy-start(s32[2,16,4]{1,2,0:T(4,128)} %param.17) | copy-start | bytes 1540
  6.5 273.4 %reduce-scatter.2.cloned.1.call-start = ((), (), s32[]{:S(2)}) async-start(), calls=%async_computation.1 | async-start | bytes 2949120 | tf_op jit(solution)/shard_map/reduce_scatter | solution.py:100
  6.5 55.8 %collective-permute-start = (bf16[1,1,2,384,768]{4,3,2,1,0:T(8,128)(2,1)}, bf16[1,1,2,384,768]{4,3,2,1,0:T(8,128)(2,1)S(1)}, u32[]{:S(2)}, u32[]{:S(2)}) collective-permute-start(bf16[1,1,2,384,768]{4,3,2,1,0:T(8,128)(2,1)} %param.11), channel_id=1, source_target_pairs={{0,16},{16,32},{32,48},{48,64},{64,80},{80,96},{96,112},{112,128},... | collective-permute-start | bytes 3538952 | tf_op jit(solution)/shard_map/ppermute | solution.py:21
  12.2 51.6 %collective-permute-start.1 = (bf16[1,1,2,384,768]{4,3,2,1,0:T(8,128)(2,1)}, bf16[1,1,2,384,768]{4,3,2,1,0:T(8,128)(2,1)S(1)}, u32[]{:S(2)}, u32[]{:S(2)}) collective-permute-start(bf16[1,1,2,384,768]{4,3,2,1,0:T(8,128)(2,1)} %param.11), channel_id=1, source_target_pairs={{16,0},{32,16},{48,32},{64,48},{80,64},{96,80},{112,96},{128,112},... | collective-permute-start | bytes 3538952 | tf_op jit(solution)/shard_map/ppermute | solution.py:22
  63.9 87.5 %collective-permute-start.2 = (bf16[3,1,2,384,768]{4,3,2,1,0:T(8,128)(2,1)S(1)}, bf16[3,1,2,384,768]{4,3,2,1,0:T(8,128)(2,1)}, u32[]{:S(2)}, u32[]{:S(2)}) collective-permute-start(bf16[3,1,2,384,768]{4,3,2,1,0:T(8,128)(2,1)S(1)} %constant_dynamic-update-slice_fusion.1), channel_id=1, source_target_pairs={{0,4},{4,8},{8,12},{1,5},{5,9},{9,13},{2,6},{6,10},{10,14},{3,7},{... | collective-permute-start | bytes 10616840 | tf_op jit(solution)/shard_map/ppermute | solution.py:21
  67.6 83.8 %collective-permute-start.3 = (bf16[3,1,2,384,768]{4,3,2,1,0:T(8,128)(2,1)S(1)}, bf16[3,1,2,384,768]{4,3,2,1,0:T(8,128)(2,1)}, u32[]{:S(2)}, u32[]{:S(2)}) collective-permute-start(bf16[3,1,2,384,768]{4,3,2,1,0:T(8,128)(2,1)S(1)} %constant_dynamic-update-slice_fusion.1), channel_id=1, source_target_pairs={{4,0},{8,4},{12,8},{5,1},{9,5},{13,9},{6,2},{10,6},{14,10},{7,3},{... | collective-permute-start | bytes 10616840 | tf_op jit(solution)/shard_map/ppermute | solution.py:22
  159.6 9.0 %copy-start = (bf16[256,768]{1,0:T(8,128)(2,1)S(1)}, bf16[256,768]{1,0:T(8,128)(2,1)}, u32[]{:S(2)}) copy-start(bf16[256,768]{1,0:T(8,128)(2,1)} %get-tuple-element.164) | copy-start | bytes 1179652
  159.6 9.0 %copy-start.1 = (bf16[256,768]{1,0:T(8,128)(2,1)S(1)}, bf16[256,768]{1,0:T(8,128)(2,1)}, u32[]{:S(2)}) copy-start(bf16[256,768]{1,0:T(8,128)(2,1)} %get-tuple-element.165) | copy-start | bytes 1179652
  168.6 9.5 %copy-start.3 = (bf16[6,384,128]{1,2,0:T(8,128)(2,1)S(1)}, bf16[6,384,128]{1,2,0:T(8,128)(2,1)}, u32[]{:S(2)}) copy-start(bf16[6,384,128]{1,2,0:T(8,128)(2,1)} %custom-call.1) | copy-start | bytes 1769476
  168.6 9.5 %copy-start.4 = (s32[6,2]{0,1:T(2,128)S(1)}, s32[6,2]{0,1:T(2,128)}, u32[]{:S(2)}) copy-start(s32[6,2]{0,1:T(2,128)} %param.16) | copy-start | bytes 148
  178.1 54.3 %copy-start.7 = (pred[384]{0:T(512)(128)(4,1)S(1)}, pred[384]{0:T(512)(128)(4,1)}, u32[]{:S(2)}) copy-start(pred[384]{0:T(512)(128)(4,1)} %and_reduce_fusion) | copy-start | bytes 1156
  232.6 47.3 %copy-start.2 = (bf16[1,1,384,768]{3,2,1,0:T(8,128)(2,1)S(1)}, bf16[1,1,384,768]{3,2,1,0:T(8,128)(2,1)}, u32[]{:S(2)}) copy-start(bf16[1,1,384,768]{3,2,1,0:T(8,128)(2,1)} %param.13) | copy-start | bytes 1769476
  232.6 47.3 %copy-start.5 = (f32[768]{0:T(1024)S(1)}, f32[768]{0:T(1024)}, u32[]{:S(2)}) copy-start(f32[768]{0:T(1024)} %param.15) | copy-start | bytes 9220
Sparse Core Ops, SparseCore 0:
  238.6 41.2 reduce-scatter.1
where the time goes:
time: 290 us; the launch traced here: 289 us
  waiting for transfers between devices  90.3 us (31%)
  blocking collectives  76.8 us (26%)
  other arithmetic  36.3 us (13%)
  matrix products  33.1 us (11%)
  local copies, waits for them, and re-layouts  21.1 us (7%)
  between operations  13.5 us (5%)
  starting transfers between devices  13.4 us (5%)
  loops' own time  4.28 us (1%)
    all_gather x1, blocking collectives, per_device(): text_both = lax.all_gather(text_kv, 'tm', axis=1, tiled=True)  76.8 us
    ppermute x2, waiting for transfers between devices, with_halo(): before = lax.ppermute(last, axis, up)  48.8 us
    reduce_scatter x1, waiting for transfers between devices, per_device(): lax.psum_scatter(projected.reshape(tiles_local, 1, tile_len, -1).astype(j...  41.4 us
    dot_general x6, matrix products, one_head(): lax.dot_general(q_head, k_head, (((1,), (1,)), ((), ())), preferred_eleme...  14.3 us
    dot_general x6, matrix products, one_head(): jnp.dot(weights.astype(jnp.bfloat16), v_head, preferred_element_type=jnp....  12.9 us
    concatenate x1, other arithmetic, one_tile(): jnp.concatenate([extended[:, :, 0].reshape(-1, col_width), text_both[0]],...  9.48 us
    ppermute x2, starting transfers between devices, with_halo(): before = lax.ppermute(last, axis, up)  9.33 us
    slice x1, local copies, waits for them, and re-layouts, one_tile(): extended[:, :, 1].reshape(-1, col_width)  8.97 us
  transfers between devices with their start and end apart: 5, of which 2 were waited for; matrix products, arithmetic and copies ran while one was open for 2% of the time, Pallas kernels for 0%

commit v1 on v0

--- a/solution.py
+++ b/solution.py
@@ -42,7 +42,15 @@
     tile_len = image_q.shape[2]
     col_width = image_q.shape[3]
     heads_here = col_width // HD
-    text_both = lax.all_gather(text_kv, "tm", axis=1, tiled=True)
+    text_both = jnp.concatenate(
+        lax.all_to_all(
+            jnp.stack([text_kv for _ in range(lax.axis_size("tm"))]),
+            axis_name="tm",
+            split_axis=0,
+            concat_axis=0,
+        ),
+        axis=1,
+    )
     extended = extend_tiles(image_kv)
     time_start = lax.axis_index("tm") * tiles_local
     height_start = lax.axis_index("height")

time: 290 us -> 259 us (0.89)
  blocking collectives: 76.8 us -> 0 us
  waiting for transfers between devices: 90.3 us -> 121 us
  starting transfers between devices: 13.4 us -> 25.1 us
    all_gather x1 -> x0, blocking collectives: 76.8 us -> none  [per_device(): text_both = lax.all_gather(text_kv, 'tm', axis=1, tiled=True)]
    all_to_all x0 -> x1, waiting for transfers between devices: none -> 32.7 us  [per_device(): lax.all_to_all(jnp.stack([text_kv for _ in range(lax.axis_size('tm'))]),...]
    all_to_all x0 -> x1, starting transfers between devices: none -> 11.7 us  [per_device(): lax.all_to_all(jnp.stack([text_kv for _ in range(lax.axis_size('tm'))]),...]
  transfers between devices with their start and end apart: 5 -> 6, of which waited for: 2 -> 3; matrix products, arithmetic and copies ran while one was open for 2% -> 3% of each run, Pallas kernels for 0% -> 0%
where the time goes in v1:
time: 259 us; the launch traced here: 258 us
  waiting for transfers between devices  121 us (47%)
  other arithmetic  36.8 us (14%)
  matrix products  33.1 us (13%)
  starting transfers between devices  25.1 us (10%)
  local copies, waits for them, and re-layouts  23.6 us (9%)
  between operations  13.6 us (5%)
  loops' own time  4.28 us (2%)
    ppermute x2, waiting for transfers between devices, with_halo(): before = lax.ppermute(last, axis, up)  48.8 us
    reduce_scatter x1, waiting for transfers between devices, per_device(): lax.psum_scatter(projected.reshape(tiles_local, 1, tile_len, -1).astype(j...  39.4 us
    all_to_all x1, waiting for transfers between devices, per_device(): lax.all_to_all(jnp.stack([text_kv for _ in range(lax.axis_size('tm'))]),...  32.7 us
    dot_general x6, matrix products, one_head(): lax.dot_general(q_head, k_head, (((1,), (1,)), ((), ())), preferred_eleme...  14.3 us
    dot_general x6, matrix products, one_head(): jnp.dot(weights.astype(jnp.bfloat16), v_head, preferred_element_type=jnp....  12.9 us
    all_to_all x1, starting transfers between devices, per_device(): lax.all_to_all(jnp.stack([text_kv for _ in range(lax.axis_size('tm'))]),...  11.7 us
    concatenate x1, other arithmetic, one_tile(): jnp.concatenate([extended[:, :, 0].reshape(-1, col_width), text_both[0]],...  9.49 us
    ppermute x2, starting transfers between devices, with_halo(): before = lax.ppermute(last, axis, up)  9.33 us
  transfers between devices with their start and end apart: 6, of which 3 were waited for; matrix products, arithmetic and copies ran while one was open for 3% of the time, Pallas kernels for 0%

profile of v1, /device:TPU:1, one launch (start us, length us, event | category | flops | bytes accessed | tf_op | source)
XLA Modules:
  0.0 257.5 jit_solution(14476114087548947664)
XLA Ops:
  6.5 5.7 %collective-permute-start = (bf16[1,1,2,384,768]{4,3,2,1,0:T(8,128)(2,1)}, bf16[1,1,2,384,768]{4,3,2,1,0:T(8,128)(2,1)S(1)}, u32[]{:S(2)}, u32[]{:S(2)}) collective-permute-start(bf16[1,1,2,384,768]{4,3,2,1,0:T(8,128)(2,1)} %param.11), channel_id=1, source_target_pairs={{0,16},{16,32},{32,48},{48,64},{64,80},{80,96},{96,112},{112,128},... | collective-permute-start | bytes 3538952 | tf_op jit(solution)/shard_map/ppermute | solution.py:21
  13.5 48.8 %collective-permute-done = bf16[1,1,2,384,768]{4,3,2,1,0:T(8,128)(2,1)S(1)} collective-permute-done((bf16[1,1,2,384,768]{4,3,2,1,0:T(8,128)(2,1)}, bf16[1,1,2,384,768]{4,3,2,1,0:T(8,128)(2,1)S(1)}, u32[]{:S(2)}, u32[]{:S(2)}) %collective-permute-start) | collective-permute-done | bytes 1179680 | tf_op jit(solution)/shard_map/ppermute | solution.py:21
  63.9 3.7 %collective-permute-start.2 = (bf16[3,1,2,384,768]{4,3,2,1,0:T(8,128)(2,1)S(1)}, bf16[3,1,2,384,768]{4,3,2,1,0:T(8,128)(2,1)}, u32[]{:S(2)}, u32[]{:S(2)}) collective-permute-start(bf16[3,1,2,384,768]{4,3,2,1,0:T(8,128)(2,1)S(1)} %constant_dynamic-update-slice_fusion.1), channel_id=1, source_target_pairs={{0,4},{4,8},{8,12},{1,5},{5,9},{9,13},{2,6},{6,10},{10,14},{3,7},{... | collective-permute-start | bytes 10616840 | tf_op jit(solution)/shard_map/ppermute | solution.py:21
  67.5 2.8 %collective-permute-start.3 = (bf16[3,1,2,384,768]{4,3,2,1,0:T(8,128)(2,1)S(1)}, bf16[3,1,2,384,768]{4,3,2,1,0:T(8,128)(2,1)}, u32[]{:S(2)}, u32[]{:S(2)}) collective-permute-start(bf16[3,1,2,384,768]{4,3,2,1,0:T(8,128)(2,1)S(1)} %constant_dynamic-update-slice_fusion.1), channel_id=1, source_target_pairs={{4,0},{8,4},{12,8},{5,1},{9,5},{13,9},{6,2},{10,6},{14,10},{7,3},{... | collective-permute-start | bytes 10616840 | tf_op jit(solution)/shard_map/ppermute | solution.py:22
  71.4 11.7 %all-to-all-start = ((bf16[16,2,16,768]{3,2,1,0:T(8,128)(2,1)}), bf16[16,2,16,768]{3,2,1,0:T(8,128)(2,1)}, u32[]{:S(2)}, u32[]{:S(2)}) async-start(bf16[16,2,16,768]{3,2,1,0:T(8,128)(2,1)} %stack.2), calls=%async_computation | async-start | bytes 1572864 | tf_op jit(solution)/shard_map/all_to_all | solution.py:46
  86.5 32.7 %all-to-all-done = bf16[16,2,16,768]{3,2,1,0:T(8,128)(2,1)} async-done(((bf16[16,2,16,768]{3,2,1,0:T(8,128)(2,1)}), bf16[16,2,16,768]{3,2,1,0:T(8,128)(2,1)}, u32[]{:S(2)}, u32[]{:S(2)}) %all-to-all-start) | async-done | bytes 786464 | tf_op jit(solution)/shard_map/all_to_all | solution.py:46
  121.2 8.2 %pad_maximum_fusion = bf16[3,3,2,384,768]{4,3,2,1,0:T(8,128)(2,1)} fusion(bf16[3,1,2,384,768]{4,3,2,1,0:T(8,128)(2,1)} %collective-permute-done.3, bf16[3,1,2,384,768]{4,3,2,1,0:T(8,128)(2,1)S(1)} %constant_dynamic-update-slice_fusion.1, bf16[3,1,2,384,768]{4,3,2,1,0:T(8,128)(2,1)} %collective-permute-done.2), kind=kLoop, calls=%fused_computation.26 | loop fusion | flops 10616832 | bytes 21233664 | tf_op jit(solution)/shard_map/concatenate | solution.py:23
  129.4 9.0 %fusion.37 = (bf16[3,3,1,384,768]{4,3,2,1,0:T(8,128)(2,1)}, bf16[3,3,1,384,768]{4,3,2,1,0:T(8,128)(2,1)}) fusion(bf16[3,3,2,384,768]{4,3,2,1,0:T(8,128)(2,1)} %pad_maximum_fusion), kind=kLoop, calls=%fused_computation.58 | loop fusion | bytes 21233664 | tf_op jit(solution)/shard_map/while/body/eval_jaxpr/slice | solution.py:71
  138.4 9.5 %pad_maximum_fusion.1 = (bf16[3712,768]{1,0:T(8,128)(2,1)}, bf16[3712,768]{1,0:T(8,128)(2,1)}) fusion(bf16[256,768]{1,0:T(8,128)(2,1)S(1)} %bitcast.34, bf16[3456,768]{1,0:T(8,128)(2,1)} %bitcast.32, bf16[256,768]{1,0:T(8,128)(2,1)S(1)} %bitcast.33, bf16[3456,768]{1,0:T(8,128)(2,1)} %bitcast.31), kind=kLoop, calls=%fused_computation.27 | loop fusion | flops 22806528 | bytes 22806528 | tf_op jit(solution)/shard_map/while/body/eval_jaxpr/concatenate | solution.py:69
  148.0 55.1 %while.19 = (s32[]{:T(128)}, bf16[6,384,128]{1,2,0:T(8,128)(2,1)S(1)}, s32[6,2]{0,1:T(2,128)S(1)}, s32[6]{0:T(128)S(1)}, bf16[384,768]{1,0:T(8,128)(2,1)}, /*ind...) while((s32[]{:T(128)}, ...), condition=%wide.region_3.4_spmd.clone.clone, body=%wide.region_0.3_spmd.clone.clone.sunk | while | flops 742752384 | bytes 19636056 | solution.py:99
  151.3 2.4 fusion.54
  154.8 2.2 fusion.56
  160.5 2.4 fusion.54
  164.0 2.2 fusion.56
  169.6 2.4 fusion.54
  173.2 2.2 fusion.56
  178.8 2.4 fusion.54
  182.4 2.2 fusion.56
  188.0 2.4 fusion.54
  191.6 2.2 fusion.56
  197.2 2.4 fusion.54
  200.8 2.2 fusion.56
  203.3 5.9 %fusion.27 = bf16[1,1,384,3072]{3,2,1,0:T(8,128)(2,1)} fusion(bf16[384,768]{0,1:T(8,128)(2,1)S(1)} %fusion.28, bf16[768,3072]{1,0:T(8,128)(2,1)} %param.14), kind=kOutput, calls=%fused_computation.30 | convolution fusion | flops 1813118976 | bytes 7667712 | tf_op jit(solution)/shard_map/dot_general | solution.py:105
  209.2 39.4 %reduce-scatter.2.cloned.1.call-done = bf16[1,1,384,768]{3,2,1,0:T(8,128)(2,1)} async-done(((bf16[1,1,384,3072]{3,2,1,0:T(8,128)(2,1)}), bf16[1,1,384,768]{3,2,1,0:T(8,128)(2,1)}) %reduce-scatter.2.cloned.1.call-update) | async-done | bytes 589840 | tf_op jit(solution)/shard_map/reduce_scatter | solution.py:108
  (100 shorter events, 35.2 us)
Async XLA Ops:
  6.5 63.9 %copy-start.4 = (bf16[2,16,768]{2,1,0:T(8,128)(2,1)S(1)}, bf16[2,16,768]{2,1,0:T(8,128)(2,1)}, u32[]{:S(2)}) copy-start(bf16[2,16,768]{2,1,0:T(8,128)(2,1)} %param.12) | copy-start | bytes 147460
  6.5 76.6 %copy-start.7 = (s32[2,16,4]{1,2,0:T(4,128)S(1)}, s32[2,16,4]{1,2,0:T(4,128)}, u32[]{:S(2)}) copy-start(s32[2,16,4]{1,2,0:T(4,128)} %param.17) | copy-start | bytes 1540
  6.5 55.8 %collective-permute-start = (bf16[1,1,2,384,768]{4,3,2,1,0:T(8,128)(2,1)}, bf16[1,1,2,384,768]{4,3,2,1,0:T(8,128)(2,1)S(1)}, u32[]{:S(2)}, u32[]{:S(2)}) collective-permute-start(bf16[1,1,2,384,768]{4,3,2,1,0:T(8,128)(2,1)} %param.11), channel_id=1, source_target_pairs={{0,16},{16,32},{32,48},{48,64},{64,80},{80,96},{96,112},{112,128},... | collective-permute-start | bytes 3538952 | tf_op jit(solution)/shard_map/ppermute | solution.py:21
  12.2 51.6 %collective-permute-start.1 = (bf16[1,1,2,384,768]{4,3,2,1,0:T(8,128)(2,1)}, bf16[1,1,2,384,768]{4,3,2,1,0:T(8,128)(2,1)S(1)}, u32[]{:S(2)}, u32[]{:S(2)}) collective-permute-start(bf16[1,1,2,384,768]{4,3,2,1,0:T(8,128)(2,1)} %param.11), channel_id=1, source_target_pairs={{16,0},{32,16},{48,32},{64,48},{80,64},{96,80},{112,96},{128,112},... | collective-permute-start | bytes 3538952 | tf_op jit(solution)/shard_map/ppermute | solution.py:22
  63.9 57.4 %collective-permute-start.2 = (bf16[3,1,2,384,768]{4,3,2,1,0:T(8,128)(2,1)S(1)}, bf16[3,1,2,384,768]{4,3,2,1,0:T(8,128)(2,1)}, u32[]{:S(2)}, u32[]{:S(2)}) collective-permute-start(bf16[3,1,2,384,768]{4,3,2,1,0:T(8,128)(2,1)S(1)} %constant_dynamic-update-slice_fusion.1), channel_id=1, source_target_pairs={{0,4},{4,8},{8,12},{1,5},{5,9},{9,13},{2,6},{6,10},{10,14},{3,7},{... | collective-permute-start | bytes 10616840 | tf_op jit(solution)/shard_map/ppermute | solution.py:21
  67.5 53.7 %collective-permute-start.3 = (bf16[3,1,2,384,768]{4,3,2,1,0:T(8,128)(2,1)S(1)}, bf16[3,1,2,384,768]{4,3,2,1,0:T(8,128)(2,1)}, u32[]{:S(2)}, u32[]{:S(2)}) collective-permute-start(bf16[3,1,2,384,768]{4,3,2,1,0:T(8,128)(2,1)S(1)} %constant_dynamic-update-slice_fusion.1), channel_id=1, source_target_pairs={{4,0},{8,4},{12,8},{5,1},{9,5},{13,9},{6,2},{10,6},{14,10},{7,3},{... | collective-permute-start | bytes 10616840 | tf_op jit(solution)/shard_map/ppermute | solution.py:22
  71.4 47.7 %all-to-all-start = ((bf16[16,2,16,768]{3,2,1,0:T(8,128)(2,1)}), bf16[16,2,16,768]{3,2,1,0:T(8,128)(2,1)}, u32[]{:S(2)}, u32[]{:S(2)}) async-start(bf16[16,2,16,768]{3,2,1,0:T(8,128)(2,1)} %stack.2), calls=%async_computation | async-start | bytes 1572864 | tf_op jit(solution)/shard_map/all_to_all | solution.py:46
  83.1 165.6 %reduce-scatter.2.cloned.1.call-start = ((), (), s32[]{:S(2)}) async-start(), calls=%async_computation.2 | async-start | bytes 2949120 | tf_op jit(solution)/shard_map/reduce_scatter | solution.py:108
  129.4 9.0 %copy-start = (bf16[1,16,16,768]{3,2,0,1:T(8,128)(2,1)S(1)}, bf16[1,16,16,768]{3,2,0,1:T(8,128)(2,1)}, u32[]{:S(2)}) copy-start(bf16[1,16,16,768]{3,2,0,1:T(8,128)(2,1)} %get-tuple-element.164) | copy-start | bytes 1179652
  129.4 9.0 %copy-start.1 = (bf16[1,16,16,768]{3,2,0,1:T(8,128)(2,1)S(1)}, bf16[1,16,16,768]{3,2,0,1:T(8,128)(2,1)}, u32[]{:S(2)}) copy-start(bf16[1,16,16,768]{3,2,0,1:T(8,128)(2,1)} %get-tuple-element.165) | copy-start | bytes 1179652
  138.4 9.5 %copy-start.3 = (bf16[6,384,128]{1,2,0:T(8,128)(2,1)S(1)}, bf16[6,384,128]{1,2,0:T(8,128)(2,1)}, u32[]{:S(2)}) copy-start(bf16[6,384,128]{1,2,0:T(8,128)(2,1)} %custom-call.1) | copy-start | bytes 1769476
  138.4 9.5 %copy-start.5 = (s32[6,2]{0,1:T(2,128)S(1)}, s32[6,2]{0,1:T(2,128)}, u32[]{:S(2)}) copy-start(s32[6,2]{0,1:T(2,128)} %param.16) | copy-start | bytes 148
  148.0 55.1 %copy-start.8 = (pred[384]{0:T(512)(128)(4,1)S(1)}, pred[384]{0:T(512)(128)(4,1)}, u32[]{:S(2)}) copy-start(pred[384]{0:T(512)(128)(4,1)} %and_reduce_fusion) | copy-start | bytes 1156
  203.3 45.4 %copy-start.2 = (bf16[1,1,384,768]{3,2,1,0:T(8,128)(2,1)S(1)}, bf16[1,1,384,768]{3,2,1,0:T(8,128)(2,1)}, u32[]{:S(2)}) copy-start(bf16[1,1,384,768]{3,2,1,0:T(8,128)(2,1)} %param.13) | copy-start | bytes 1769476
  203.3 45.3 %copy-start.6 = (f32[768]{0:T(1024)S(1)}, f32[768]{0:T(1024)}, u32[]{:S(2)}) copy-start(f32[768]{0:T(1024)} %param.15) | copy-start | bytes 9220
Sparse Core Ops, SparseCore 0:
  209.3 39.2 reduce-scatter.1
